TPU v7x, 256 devices: a whole 4x4x8 slice. The times are simulated.
256 devices in a mesh: dom: 16 (over z, core), grp: 16 (over y, x).
Axes of the slice: x: 4, y: 4, z: 8, core: 2. Of those that a mesh axis runs over, the one named last changes fastest.
Arguments:
- positions: float32 [65536, 3, 128], P(('dom', 'grp')), may hold values from -4 to 4
- velocities: float32 [65536, 3, 128], P(('dom', 'grp')), may hold values from -9 to 9
- masses: float32 [65536, 128], P(('dom', 'grp')), may hold values from 0.3 to 3
- destination: int32 [65536], P(('dom', 'grp')), may hold values from 0 to 15, as said below
- group_ids: int32 [65536, 128], P(('dom', 'grp')), may hold values from 0 to 1023, as said below
- boundary_set: int32 [256, 64], P(('dom', 'grp')), may hold values from 0 to 511, as said below
- send_list: int32 [256, 16, 16], P(('dom', 'grp')), may hold values from 0 to 63, as said below
- send_count: int32 [256, 16], P(('dom', 'grp')), may hold values from 0 to 16, as said below
- partners: int32 [131072, 4], P(('dom', 'grp')), may hold values from 0 to 767, as said below
Outputs:
- energy: float32 [65536, 128], P(('dom', 'grp'))
- group_kinetic: float32 [1024], replicated
Inputs may be any that keep to these rules, and one draw needn't show every extreme that they name: Each block of 256 leaves sends at most 32 leaves to one destination; in each dom index one destination receives exactly 32 leaves from every block. `group_ids`: the particles of block b carry the 16 group numbers 4 * b to 4 * b + 15, taken modulo 1024, each at least once and no others. `boundary_set`: each row holds 64 distinct slot numbers. `send_list`: each row of 16 holds distinct positions. `send_count`: A block sends nothing to its own grp index; in each dom index one grp index receives 16 from every other block. `partners`: each row holds 4 distinct entry numbers of combined.
All inputs are finite; a program needn't handle non-finite values.
Results may differ from a plain program's by a relative error of at most 0.0003.
Values sent between devices are 32-bit elements; how exact they have to be, the bound alone decides.
No kernel may reach another device: no remote copies, remote signals or barrier semaphores. Data moves between devices by JAX's collectives and lax.ppermute only.
A program may use at most 64 MiB of HBM per device.

v0:
```python
import jax
import jax.numpy as jnp
from jax import lax
from jax.sharding import PartitionSpec as P

GSPAN = 16
GROUP_DEV = 4
softening = 0.0025
exact = lax.Precision.HIGHEST


def select_rows(table, index):
    count = table.shape[0]
    flat = table.reshape(count, -1)
    picker = (index.reshape(-1)[:, None] == jnp.arange(count, dtype=jnp.int32)[None, :]).astype(
        jnp.float32
    )
    chosen = jnp.dot(picker, flat, precision=exact, preferred_element_type=jnp.float32)
    return chosen.reshape(index.shape + table.shape[1:])


def tile_potential(targets, sources):
    distance = softening
    for component in range(3):
        offset = targets[:, None, component, :, None] - sources[:, :, component, None, :]
        distance = distance + offset * offset
    weights = sources[:, :, 3, None, :] * lax.rsqrt(distance)
    return -jnp.sum(weights, axis=(1, 3))


def slot_potential(owned, combined, pair_index, coupling):
    slot_count = owned.shape[0]
    leaf_width = owned.shape[2]
    block_rows = max(32, slot_count // 16)

    def one_block(inputs):
        targets, indices = inputs
        sources = select_rows(combined, indices)
        return tile_potential(targets, sources)

    result = lax.map(
        one_block,
        (
            owned.reshape(slot_count // block_rows, block_rows, 4, leaf_width),
            pair_index.reshape(slot_count // block_rows, block_rows, pair_index.shape[1]),
        ),
    )
    return result.reshape(slot_count, leaf_width) * coupling


def shards(
    positions,
    velocities,
    masses,
    destination,
    group_ids,
    boundary_set,
    send_list,
    send_count,
    partners,
):
    owners = lax.axis_size("grp")
    leaves = positions.shape[0]
    leaf_width = positions.shape[2]
    capacity = 2 * leaves // owners
    slot_count = owners * capacity
    groups = GROUP_DEV * lax.axis_size("dom") * owners
    block_index = lax.axis_index("dom") * owners + lax.axis_index("grp")
    first_group = block_index * GROUP_DEV
    mass_flat = masses.reshape(-1)
    group_flat = group_ids.reshape(-1)
    speeds = jnp.transpose(velocities, (1, 0, 2)).reshape(3, -1)
    local_ids = (group_flat - first_group) % groups
    member = (jnp.arange(GSPAN, dtype=jnp.int32)[:, None] == local_ids[None, :]).astype(jnp.float32)
    place = (
        (first_group + jnp.arange(GSPAN, dtype=jnp.int32))[:, None] % groups
        == jnp.arange(groups, dtype=jnp.int32)[None, :]
    ).astype(jnp.float32)

    def group_sums(stats):
        local_sums = jnp.einsum(
            "kp,gp->kg", stats, member, precision=exact, preferred_element_type=jnp.float32
        )
        return jnp.dot(local_sums, place, precision=exact, preferred_element_type=jnp.float32)

    first_sums = group_sums(
        jnp.concatenate([mass_flat[None, :], mass_flat[None, :] * speeds], axis=0)
    )
    mass_total, momentum = lax.psum((first_sums[0], first_sums[1:]), ("dom", "grp"))
    bulk_velocity = momentum / mass_total[None, :]
    bulk_local = jnp.einsum(
        "kq,gq->kg", bulk_velocity, place, precision=exact, preferred_element_type=jnp.float32
    )
    per_particle = jnp.dot(bulk_local, member, precision=exact, preferred_element_type=jnp.float32)
    relative = speeds - per_particle
    kinetic = 0.5 * jnp.sum(relative * relative, axis=0)
    heat_sum = lax.psum(group_sums((mass_flat * kinetic)[None, :])[0], ("dom", "grp"))
    group_kinetic = heat_sum / mass_total
    onehot = (destination[:, None] == jnp.arange(owners, dtype=jnp.int32)[None, :]).astype(
        jnp.int32
    )
    leaf_rank = jnp.sum((jnp.cumsum(onehot, axis=0) - onehot) * onehot, axis=1)
    target = destination * capacity + leaf_rank
    payload = jnp.concatenate([positions, masses[:, None, :]], axis=1)
    placing = (jnp.arange(slot_count, dtype=jnp.int32)[:, None] == target[None, :]).astype(
        jnp.float32
    )
    outgoing = jnp.dot(
        placing, payload.reshape(leaves, -1), precision=exact, preferred_element_type=jnp.float32
    ).reshape(slot_count, 4, leaf_width)
    owned = lax.all_to_all(outgoing, "grp", split_axis=0, concat_axis=0, tiled=True)
    set_size = boundary_set.shape[1]
    per_peer = send_list.shape[2]
    boundary = select_rows(owned, boundary_set[0])
    every_set = lax.all_gather(boundary, "grp", axis=0, tiled=True)
    all_lists, all_counts = (
        lax.all_gather(send_list, "grp", axis=0, tiled=True),
        lax.all_gather(send_count, "grp", axis=0, tiled=True),
    )
    my_index = lax.axis_index("grp")
    my_lists = jnp.take(all_lists, my_index, axis=1)
    my_counts = jnp.take(all_counts, my_index, axis=1)
    positions_in = jnp.arange(owners, dtype=jnp.int32)[:, None] * set_size + my_lists
    remote = select_rows(every_set, positions_in)
    is_live = jnp.arange(per_peer, dtype=jnp.int32)[None, :] < my_counts[:, None]
    remote = jnp.where(is_live[:, :, None, None], remote, jnp.zeros_like(remote))
    remote = remote.reshape(owners * per_peer, 4, leaf_width)
    combined = jnp.concatenate([owned, remote], axis=0)
    coupling = 1.0 / (partners.shape[1] * leaf_width)
    potential = slot_potential(owned, combined, partners, coupling)
    returned = lax.all_to_all(potential, "grp", split_axis=0, concat_axis=0, tiled=True)
    own_potential = jnp.einsum(
        "sl,sp->lp", placing, returned, precision=exact, preferred_element_type=jnp.float32
    )
    energy = kinetic.reshape(leaves, leaf_width) + own_potential
    return (energy, group_kinetic)


def solution(mesh):
    in_specs = (
        P(("dom", "grp"), None, None),
        P(("dom", "grp"), None, None),
        P(("dom", "grp"), None),
        P(("dom", "grp")),
        P(("dom", "grp"), None),
        P(("dom", "grp"), None),
        P(("dom", "grp"), None, None),
        P(("dom", "grp"), None),
        P(("dom", "grp"), None),
    )
    out_specs = (P(("dom", "grp"), None), P())
    return jax.shard_map(shards, mesh=mesh, in_specs=in_specs, out_specs=out_specs, check_vma=False)
```

profile of v0, /device:TPU:1, one launch (start us, length us, event | category | flops | bytes accessed | tf_op | source)
XLA Modules:
  0.0 366.0 jit_solution(14305169449429546651)
XLA Ops:
  10.2 1.2 copy.63
  13.7 23.4 %all_to_all.14 = f32[512,4,128]{2,1,0:T(4,128)S(1)} all-to-all(f32[512,4,128]{2,1,0:T(4,128)S(1)} %copy.64), channel_id=1, replica_groups=mesh['dom'=16,'grp'=16] {'grp'}, dimensions={0} | all-to-all | bytes 2097152 | tf_op jit(solution)/shard_map/all_to_all | solution.py:111
  37.5 1.4 fusion.15
  39.4 1.6 fusion.9
  42.0 14.1 %all-gather = s32[16,1,16]{2,1,0:T(1,128)S(1)} all-gather(s32[1,1,16]{2,1,0:T(1,128)S(1)} %bitcast.158), channel_id=1, replica_groups=mesh['dom'=16,'grp'=16] {'grp'}, dimensions={0}, use_global_device_ids=true | all-gather | bytes 1088 | tf_op jit(solution)/shard_map/all_gather | solution.py:118
  56.6 17.3 %all_gather.10 = s32[16,16,16]{2,1,0:T(8,128)S(1)} all-gather(s32[1,16,16]{2,1,0:T(8,128)S(1)} %copy-done.7), channel_id=1, replica_groups=mesh['dom'=16,'grp'=16] {'grp'}, dimensions={0}, use_global_device_ids=true | all-gather | bytes 17408 | tf_op jit(solution)/shard_map/all_gather | solution.py:117
  73.9 89.0 %all-reduce = (f32[3,1024]{1,0:T(4,128)S(1)}, f32[1024]{0:T(1024)S(1)}) all-reduce(f32[3,1024]{1,0:T(4,128)S(1)} %slice.60, f32[1024]{0:T(1024)S(1)} %bitcast.154), channel_id=1, replica_groups=mesh['dom'=16,'grp'=16] {'dom','grp'}, use_global_device_ids=true, to_apply=%region_0.1 | all-reduce | flops 4096 | bytes 32768 | tf_op jit(solution)/shard_map/psum | solution.py:89
  163.1 1.1 fusion.13
  165.0 1.9 copy.66
  166.9 1.3 fusion.10
  168.6 1.5 pad_maximum_fusion
  170.1 1.7 copy.70
  171.8 104.0 %while.12 = (s32[]{:T(128)}, f32[16,32,128]{2,1,0:T(8,128)S(1)}, s32[16,32,4]{1,0,2:T(8,128)}, f32[768,4,128]{0,2,1:T(8,128)S(1)}, f32[16,32,4,128]{3,2,1,0:T(4,128)S(1)}, /*index=5*/s32[]{:T(128)}) while((s32[]{:T(128)}, f32[16,32,128]{2,1,0:T(8,128)S(1)}, s32[16,32,4]{1,0,2:T(8,128)}, f32[768,4,128]{0,2,1:T(8,128)S(1)}, ...), condition=%wide.region_8.9_spmd, body=%wide.region_6.8_spmd.sunk | while | flops 627146752 | bytes 3606097 | solution.py:41
  172.7 1.0 fusion.63
  174.0 4.4 %multiply_reduce_fusion.2 = f32[32,128]{1,0:T(8,128)S(1)} fusion(f32[32,4,128]{2,1,0:T(4,128)S(1)} %copy.88, f32[32,128]{1,0:T(8,128)S(1)} %get-tuple-element.135, f32[32,4,128]{2,1,0:T(4,128)S(1)} %copy.90, f32[32,128]{1,0:T(8,128)S(1)} %get-tuple-element.137, f32[32,4,128]{2,1,0:T(4,128)S(1)} %copy.91, f32[32,128]{1,0:T(8,128)S(1)} %get-tuple-element.139, ...), kind=kLoop, calls=%fused_computation.clone.1 | loop fusion | flops 23064576 | bytes 327680 | tf_op jit(solution)/shard_map/while/body/eval_jaxpr/reduce_sum | solution.py:28
  179.1 1.0 fusion.63
  180.5 4.4 %multiply_reduce_fusion.2 = f32[32,128]{1,0:T(8,128)S(1)} fusion(f32[32,4,128]{2,1,0:T(4,128)S(1)} %copy.88, f32[32,128]{1,0:T(8,128)S(1)} %get-tuple-element.135, f32[32,4,128]{2,1,0:T(4,128)S(1)} %copy.90, f32[32,128]{1,0:T(8,128)S(1)} %get-tuple-element.137, f32[32,4,128]{2,1,0:T(4,128)S(1)} %copy.91, f32[32,128]{1,0:T(8,128)S(1)} %get-tuple-element.139, ...), kind=kLoop, calls=%fused_computation.clone.1 | loop fusion | flops 23064576 | bytes 327680 | tf_op jit(solution)/shard_map/while/body/eval_jaxpr/reduce_sum | solution.py:28
  185.6 1.0 fusion.63
  187.0 4.4 %multiply_reduce_fusion.2 = f32[32,128]{1,0:T(8,128)S(1)} fusion(f32[32,4,128]{2,1,0:T(4,128)S(1)} %copy.88, f32[32,128]{1,0:T(8,128)S(1)} %get-tuple-element.135, f32[32,4,128]{2,1,0:T(4,128)S(1)} %copy.90, f32[32,128]{1,0:T(8,128)S(1)} %get-tuple-element.137, f32[32,4,128]{2,1,0:T(4,128)S(1)} %copy.91, f32[32,128]{1,0:T(8,128)S(1)} %get-tuple-element.139, ...), kind=kLoop, calls=%fused_computation.clone.1 | loop fusion | flops 23064576 | bytes 327680 | tf_op jit(solution)/shard_map/while/body/eval_jaxpr/reduce_sum | solution.py:28
  192.1 1.0 fusion.63
  193.5 4.4 %multiply_reduce_fusion.2 = f32[32,128]{1,0:T(8,128)S(1)} fusion(f32[32,4,128]{2,1,0:T(4,128)S(1)} %copy.88, f32[32,128]{1,0:T(8,128)S(1)} %get-tuple-element.135, f32[32,4,128]{2,1,0:T(4,128)S(1)} %copy.90, f32[32,128]{1,0:T(8,128)S(1)} %get-tuple-element.137, f32[32,4,128]{2,1,0:T(4,128)S(1)} %copy.91, f32[32,128]{1,0:T(8,128)S(1)} %get-tuple-element.139, ...), kind=kLoop, calls=%fused_computation.clone.1 | loop fusion | flops 23064576 | bytes 327680 | tf_op jit(solution)/shard_map/while/body/eval_jaxpr/reduce_sum | solution.py:28
  198.6 1.0 fusion.63
  200.0 4.4 %multiply_reduce_fusion.2 = f32[32,128]{1,0:T(8,128)S(1)} fusion(f32[32,4,128]{2,1,0:T(4,128)S(1)} %copy.88, f32[32,128]{1,0:T(8,128)S(1)} %get-tuple-element.135, f32[32,4,128]{2,1,0:T(4,128)S(1)} %copy.90, f32[32,128]{1,0:T(8,128)S(1)} %get-tuple-element.137, f32[32,4,128]{2,1,0:T(4,128)S(1)} %copy.91, f32[32,128]{1,0:T(8,128)S(1)} %get-tuple-element.139, ...), kind=kLoop, calls=%fused_computation.clone.1 | loop fusion | flops 23064576 | bytes 327680 | tf_op jit(solution)/shard_map/while/body/eval_jaxpr/reduce_sum | solution.py:28
  205.1 1.0 fusion.63
  206.5 4.4 %multiply_reduce_fusion.2 = f32[32,128]{1,0:T(8,128)S(1)} fusion(f32[32,4,128]{2,1,0:T(4,128)S(1)} %copy.88, f32[32,128]{1,0:T(8,128)S(1)} %get-tuple-element.135, f32[32,4,128]{2,1,0:T(4,128)S(1)} %copy.90, f32[32,128]{1,0:T(8,128)S(1)} %get-tuple-element.137, f32[32,4,128]{2,1,0:T(4,128)S(1)} %copy.91, f32[32,128]{1,0:T(8,128)S(1)} %get-tuple-element.139, ...), kind=kLoop, calls=%fused_computation.clone.1 | loop fusion | flops 23064576 | bytes 327680 | tf_op jit(solution)/shard_map/while/body/eval_jaxpr/reduce_sum | solution.py:28
  213.0 4.4 %multiply_reduce_fusion.2 = f32[32,128]{1,0:T(8,128)S(1)} fusion(f32[32,4,128]{2,1,0:T(4,128)S(1)} %copy.88, f32[32,128]{1,0:T(8,128)S(1)} %get-tuple-element.135, f32[32,4,128]{2,1,0:T(4,128)S(1)} %copy.90, f32[32,128]{1,0:T(8,128)S(1)} %get-tuple-element.137, f32[32,4,128]{2,1,0:T(4,128)S(1)} %copy.91, f32[32,128]{1,0:T(8,128)S(1)} %get-tuple-element.139, ...), kind=kLoop, calls=%fused_computation.clone.1 | loop fusion | flops 23064576 | bytes 327680 | tf_op jit(solution)/shard_map/while/body/eval_jaxpr/reduce_sum | solution.py:28
  218.1 1.0 fusion.63
  219.4 4.4 %multiply_reduce_fusion.2 = f32[32,128]{1,0:T(8,128)S(1)} fusion(f32[32,4,128]{2,1,0:T(4,128)S(1)} %copy.88, f32[32,128]{1,0:T(8,128)S(1)} %get-tuple-element.135, f32[32,4,128]{2,1,0:T(4,128)S(1)} %copy.90, f32[32,128]{1,0:T(8,128)S(1)} %get-tuple-element.137, f32[32,4,128]{2,1,0:T(4,128)S(1)} %copy.91, f32[32,128]{1,0:T(8,128)S(1)} %get-tuple-element.139, ...), kind=kLoop, calls=%fused_computation.clone.1 | loop fusion | flops 23064576 | bytes 327680 | tf_op jit(solution)/shard_map/while/body/eval_jaxpr/reduce_sum | solution.py:28
  224.6 1.0 fusion.63
  225.9 4.4 %multiply_reduce_fusion.2 = f32[32,128]{1,0:T(8,128)S(1)} fusion(f32[32,4,128]{2,1,0:T(4,128)S(1)} %copy.88, f32[32,128]{1,0:T(8,128)S(1)} %get-tuple-element.135, f32[32,4,128]{2,1,0:T(4,128)S(1)} %copy.90, f32[32,128]{1,0:T(8,128)S(1)} %get-tuple-element.137, f32[32,4,128]{2,1,0:T(4,128)S(1)} %copy.91, f32[32,128]{1,0:T(8,128)S(1)} %get-tuple-element.139, ...), kind=kLoop, calls=%fused_computation.clone.1 | loop fusion | flops 23064576 | bytes 327680 | tf_op jit(solution)/shard_map/while/body/eval_jaxpr/reduce_sum | solution.py:28
  231.1 1.0 fusion.63
  232.4 4.4 %multiply_reduce_fusion.2 = f32[32,128]{1,0:T(8,128)S(1)} fusion(f32[32,4,128]{2,1,0:T(4,128)S(1)} %copy.88, f32[32,128]{1,0:T(8,128)S(1)} %get-tuple-element.135, f32[32,4,128]{2,1,0:T(4,128)S(1)} %copy.90, f32[32,128]{1,0:T(8,128)S(1)} %get-tuple-element.137, f32[32,4,128]{2,1,0:T(4,128)S(1)} %copy.91, f32[32,128]{1,0:T(8,128)S(1)} %get-tuple-element.139, ...), kind=kLoop, calls=%fused_computation.clone.1 | loop fusion | flops 23064576 | bytes 327680 | tf_op jit(solution)/shard_map/while/body/eval_jaxpr/reduce_sum | solution.py:28
  237.6 1.0 fusion.63
  238.9 4.4 %multiply_reduce_fusion.2 = f32[32,128]{1,0:T(8,128)S(1)} fusion(f32[32,4,128]{2,1,0:T(4,128)S(1)} %copy.88, f32[32,128]{1,0:T(8,128)S(1)} %get-tuple-element.135, f32[32,4,128]{2,1,0:T(4,128)S(1)} %copy.90, f32[32,128]{1,0:T(8,128)S(1)} %get-tuple-element.137, f32[32,4,128]{2,1,0:T(4,128)S(1)} %copy.91, f32[32,128]{1,0:T(8,128)S(1)} %get-tuple-element.139, ...), kind=kLoop, calls=%fused_computation.clone.1 | loop fusion | flops 23064576 | bytes 327680 | tf_op jit(solution)/shard_map/while/body/eval_jaxpr/reduce_sum | solution.py:28
  244.1 1.0 fusion.63
  245.4 4.4 %multiply_reduce_fusion.2 = f32[32,128]{1,0:T(8,128)S(1)} fusion(f32[32,4,128]{2,1,0:T(4,128)S(1)} %copy.88, f32[32,128]{1,0:T(8,128)S(1)} %get-tuple-element.135, f32[32,4,128]{2,1,0:T(4,128)S(1)} %copy.90, f32[32,128]{1,0:T(8,128)S(1)} %get-tuple-element.137, f32[32,4,128]{2,1,0:T(4,128)S(1)} %copy.91, f32[32,128]{1,0:T(8,128)S(1)} %get-tuple-element.139, ...), kind=kLoop, calls=%fused_computation.clone.1 | loop fusion | flops 23064576 | bytes 327680 | tf_op jit(solution)/shard_map/while/body/eval_jaxpr/reduce_sum | solution.py:28
  250.6 1.0 fusion.63
  251.9 4.4 %multiply_reduce_fusion.2 = f32[32,128]{1,0:T(8,128)S(1)} fusion(f32[32,4,128]{2,1,0:T(4,128)S(1)} %copy.88, f32[32,128]{1,0:T(8,128)S(1)} %get-tuple-element.135, f32[32,4,128]{2,1,0:T(4,128)S(1)} %copy.90, f32[32,128]{1,0:T(8,128)S(1)} %get-tuple-element.137, f32[32,4,128]{2,1,0:T(4,128)S(1)} %copy.91, f32[32,128]{1,0:T(8,128)S(1)} %get-tuple-element.139, ...), kind=kLoop, calls=%fused_computation.clone.1 | loop fusion | flops 23064576 | bytes 327680 | tf_op jit(solution)/shard_map/while/body/eval_jaxpr/reduce_sum | solution.py:28
  257.1 1.0 fusion.63
  258.4 4.4 %multiply_reduce_fusion.2 = f32[32,128]{1,0:T(8,128)S(1)} fusion(f32[32,4,128]{2,1,0:T(4,128)S(1)} %copy.88, f32[32,128]{1,0:T(8,128)S(1)} %get-tuple-element.135, f32[32,4,128]{2,1,0:T(4,128)S(1)} %copy.90, f32[32,128]{1,0:T(8,128)S(1)} %get-tuple-element.137, f32[32,4,128]{2,1,0:T(4,128)S(1)} %copy.91, f32[32,128]{1,0:T(8,128)S(1)} %get-tuple-element.139, ...), kind=kLoop, calls=%fused_computation.clone.1 | loop fusion | flops 23064576 | bytes 327680 | tf_op jit(solution)/shard_map/while/body/eval_jaxpr/reduce_sum | solution.py:28
  263.6 1.0 fusion.63
  264.9 4.4 %multiply_reduce_fusion.2 = f32[32,128]{1,0:T(8,128)S(1)} fusion(f32[32,4,128]{2,1,0:T(4,128)S(1)} %copy.88, f32[32,128]{1,0:T(8,128)S(1)} %get-tuple-element.135, f32[32,4,128]{2,1,0:T(4,128)S(1)} %copy.90, f32[32,128]{1,0:T(8,128)S(1)} %get-tuple-element.137, f32[32,4,128]{2,1,0:T(4,128)S(1)} %copy.91, f32[32,128]{1,0:T(8,128)S(1)} %get-tuple-element.139, ...), kind=kLoop, calls=%fused_computation.clone.1 | loop fusion | flops 23064576 | bytes 327680 | tf_op jit(solution)/shard_map/while/body/eval_jaxpr/reduce_sum | solution.py:28
  270.0 1.0 fusion.63
  271.4 4.4 %multiply_reduce_fusion.2 = f32[32,128]{1,0:T(8,128)S(1)} fusion(f32[32,4,128]{2,1,0:T(4,128)S(1)} %copy.88, f32[32,128]{1,0:T(8,128)S(1)} %get-tuple-element.135, f32[32,4,128]{2,1,0:T(4,128)S(1)} %copy.90, f32[32,128]{1,0:T(8,128)S(1)} %get-tuple-element.137, f32[32,4,128]{2,1,0:T(4,128)S(1)} %copy.91, f32[32,128]{1,0:T(8,128)S(1)} %get-tuple-element.139, ...), kind=kLoop, calls=%fused_computation.clone.1 | loop fusion | flops 23064576 | bytes 327680 | tf_op jit(solution)/shard_map/while/body/eval_jaxpr/reduce_sum | solution.py:28
  276.5 3.5 all-to-all-start.1
  280.1 1.4 fusion.14
  281.7 75.6 %psum.23 = f32[1024]{0:T(1024)S(1)} all-reduce(f32[1024]{0:T(1024)S(1)} %bitcast.156), channel_id=1, replica_groups=mesh['dom'=16,'grp'=16] {'dom','grp'}, use_global_device_ids=true, to_apply=%region_9.10 | all-reduce | flops 1024 | bytes 8192 | tf_op jit(solution)/shard_map/psum | solution.py:97
  357.9 1.3 convolution_add_fusion
  (224 shorter events, 27.0 us)
Async XLA Ops:
  7.2 157.8 %all-gather.3.cloned.1.call-start = ((), (), s32[]{:S(2)}) async-start(), calls=%async_computation.2 | async-start | bytes 2228224 | tf_op jit(solution)/shard_map/all_gather | solution.py:115
  13.7 23.8 %copy-start.10 = (s32[1,64]{1,0:T(1,128)S(1)}, s32[1,64]{1,0:T(1,128)}, u32[]{:S(2)}) copy-start(s32[1,64]{1,0:T(1,128)} %param.16) | copy-start | bytes 772
  37.1 1.8 copy-start
  37.1 1.8 copy-start.1
  37.1 2.2 copy-start.3
  37.5 3.8 %copy-start.6 = (s32[512,4]{0,1:T(4,128)S(1)}, s32[512,4]{0,1:T(4,128)}, u32[]{:S(2)}) copy-start(s32[512,4]{0,1:T(4,128)} %param.19) | copy-start | bytes 24580
  37.5 4.5 %copy-start.11 = (s32[1,16]{1,0:T(1,128)S(1)}, s32[1,16]{1,0:T(1,128)}, u32[]{:S(2)}) copy-start(s32[1,16]{1,0:T(1,128)} %param.18) | copy-start | bytes 196
  37.5 19.0 %copy-start.7 = (s32[1,16,16]{2,1,0:T(8,128)S(1)}, s32[1,16,16]{2,1,0:T(8,128)}, u32[]{:S(2)}) copy-start(s32[1,16,16]{2,1,0:T(8,128)} %param.17) | copy-start | bytes 3076
  39.3 125.7 %copy-start.12 = (s32[16]{0:T(128)}, s32[16]{0:T(128)S(1)}, u32[]{:S(2)}) copy-start(s32[16]{0:T(128)S(1)} %and_select_fusion) | copy-start | bytes 196
  39.4 125.6 %copy-start.4 = (s32[32768]{0:T(1024)}, s32[32768]{0:T(1024)S(1)}, u32[]{:S(2)}) copy-start(s32[32768]{0:T(1024)S(1)} %add_select_fusion) | copy-start | bytes 393220
  162.8 1.4 copy-start.8
  171.8 108.3 %copy-start.2 = (f32[32768]{0:T(1024)S(1)}, f32[32768]{0:T(1024)}, u32[]{:S(2)}) copy-start(f32[32768]{0:T(1024)} %multiply_multiply_fusion) | copy-start | bytes 393220
  171.8 108.3 %copy-start.5 = (s32[32768]{0:T(1024)S(1)}, s32[32768]{0:T(1024)}, u32[]{:S(2)}) copy-start(s32[32768]{0:T(1024)} %copy-done.4) | copy-start | bytes 393220
  171.8 109.7 %copy-start.13 = (s32[16]{0:T(128)S(1)}, s32[16]{0:T(128)}, u32[]{:S(2)}) copy-start(s32[16]{0:T(128)} %copy-done.12) | copy-start | bytes 196
  171.8 185.5 %copy-start.9 = (f32[1024]{0:T(1024)S(1)}, f32[1024]{0:T(1024)}, u32[]{:S(2)}) copy-start(f32[1024]{0:T(1024)} %copy-done.8) | copy-start | bytes 12292
  276.5 81.4 %all-to-all-start.1 = ((f32[16,32,128]{2,1,0:T(8,128)}), f32[16,32,128]{2,1,0:T(8,128)S(1)}, u32[]{:S(2)}, u32[]{:S(2)}) async-start(f32[16,32,128]{2,1,0:T(8,128)} %broadcast_multiply_fusion), calls=%async_computation.1 | async-start | bytes 524288 | tf_op jit(solution)/shard_map/all_to_all | solution.py:131
Sparse Core Ops, SparseCore 0:
  39.0 48.9 all-gather.2
where the time goes:
time: 367 us; the launch traced here: 366 us
  blocking collectives  219 us (60%)
  other arithmetic  77.5 us (21%)
  matrix products  26 us (7%)
  local copies, waits for them, and re-layouts  23.5 us (6%)
  between operations  14.4 us (4%)
    psum x1, blocking collectives, shards(): lax.psum((first_sums[0], first_sums[1:]), ('dom', 'grp'))  89 us
    psum x1, blocking collectives, shards(): lax.psum(group_sums((mass_flat * kinetic)[None, :])[0], ('dom', 'grp'))  75.6 us
    reduce_sum x16, other arithmetic, tile_potential(): return -jnp.sum(weights, axis=(1, 3))  70.1 us
    all_to_all x1, blocking collectives, shards(): lax.all_to_all(outgoing, 'grp', split_axis=0, concat_axis=0, tiled=True)  23.4 us
    dot_general x18, matrix products, select_rows(): jnp.dot(picker, flat, precision=exact, preferred_element_type=jnp.float32)  19.3 us
    all_gather x1, blocking collectives, shards(): lax.all_gather(send_list, 'grp', axis=0, tiled=True)  17.3 us
    all_gather x1, blocking collectives, shards(): lax.all_gather(send_count, 'grp', axis=0, tiled=True)  14.1 us
    dynamic_slice x48, local copies, waits for them, and re-layouts, slot_potential(): lax.map(one_block, (owned.reshape(slot_count // block_rows, block_rows, 4...  12.1 us
  transfers between devices with their start and end apart: 2, of which 0 were waited for; matrix products, arithmetic and copies ran while one was open for 2% of the time, Pallas kernels for 0%

commit v1 on v0

--- a/solution.py
+++ b/solution.py
@@ -115,7 +115,9 @@
     every_set = lax.all_gather(boundary, "grp", axis=0, tiled=True)
     all_lists, all_counts = (
         lax.all_gather(send_list, "grp", axis=0, tiled=True),
-        lax.all_gather(send_count, "grp", axis=0, tiled=True),
+        jnp.concatenate(
+            lax.all_to_all(jnp.stack([send_count] * lax.axis_size("grp")), "grp", 0, 0), axis=0
+        ),
     )
     my_index = lax.axis_index("grp")
     my_lists = jnp.take(all_lists, my_index, axis=1)

time: 367 us -> 355 us (0.967)
  blocking collectives: 219 us -> 203 us
    all_gather x1 -> x0, blocking collectives: 14.1 us -> none  [shards(): lax.all_gather(send_count, 'grp', axis=0, tiled=True)]
  transfers between devices with their start and end apart: 2 -> 3, of which waited for: 0 -> 0; matrix products, arithmetic and copies ran while one was open for 2% -> 3% of each run, Pallas kernels for 0% -> 0%
where the time goes in v1:
time: 355 us; the launch traced here: 354 us
  blocking collectives  203 us (57%)
  other arithmetic  77.5 us (22%)
  matrix products  26 us (7%)
  local copies, waits for them, and re-layouts  24.1 us (7%)
  between operations  14.4 us (4%)
  starting transfers between devices  7.06 us (2%)
    psum x1, blocking collectives, shards(): lax.psum((first_sums[0], first_sums[1:]), ('dom', 'grp'))  85.8 us
    psum x1, blocking collectives, shards(): lax.psum(group_sums((mass_flat * kinetic)[None, :])[0], ('dom', 'grp'))  75.6 us
    reduce_sum x16, other arithmetic, tile_potential(): return -jnp.sum(weights, axis=(1, 3))  70.1 us
    all_to_all x1, blocking collectives, shards(): lax.all_to_all(outgoing, 'grp', split_axis=0, concat_axis=0, tiled=True)  23.4 us
    dot_general x18, matrix products, select_rows(): jnp.dot(picker, flat, precision=exact, preferred_element_type=jnp.float32)  19.3 us
    all_gather x1, blocking collectives, shards(): lax.all_gather(send_list, 'grp', axis=0, tiled=True)  18.4 us
    dynamic_slice x48, local copies, waits for them, and re-layouts, slot_potential(): lax.map(one_block, (owned.reshape(slot_count // block_rows, block_rows, 4...  12.1 us
  transfers between devices with their start and end apart: 3, of which 0 were waited for; matrix products, arithmetic and copies ran while one was open for 3% of the time, Pallas kernels for 0%

profile of v1, /device:TPU:1, one launch (start us, length us, event | category | flops | bytes accessed | tf_op | source)
XLA Modules:
  0.0 354.0 jit_solution(12538834795533487769)
XLA Ops:
  10.1 1.2 copy.63
  13.6 23.4 %all_to_all.19 = f32[512,4,128]{2,1,0:T(4,128)S(1)} all-to-all(f32[512,4,128]{2,1,0:T(4,128)S(1)} %copy.64), channel_id=1, replica_groups=mesh['dom'=16,'grp'=16] {'grp'}, dimensions={0} | all-to-all | bytes 2097152 | tf_op jit(solution)/shard_map/all_to_all | solution.py:111
  37.7 3.5 all-to-all-start.1
  41.6 1.4 fusion.15
  43.5 1.6 fusion.9
  45.4 18.4 %all_gather.6 = s32[16,16,16]{2,1,0:T(8,128)S(1)} all-gather(s32[1,16,16]{2,1,0:T(8,128)S(1)} %copy-done.6), channel_id=1, replica_groups=mesh['dom'=16,'grp'=16] {'grp'}, dimensions={0}, use_global_device_ids=true | all-gather | bytes 17408 | tf_op jit(solution)/shard_map/all_gather | solution.py:117
  63.8 85.8 %all-reduce = (f32[3,1024]{1,0:T(4,128)S(1)}, f32[1024]{0:T(1024)S(1)}) all-reduce(f32[3,1024]{1,0:T(4,128)S(1)} %slice.60, f32[1024]{0:T(1024)S(1)} %bitcast.154), channel_id=1, replica_groups=mesh['dom'=16,'grp'=16] {'dom','grp'}, use_global_device_ids=true, to_apply=%region_0.1 | all-reduce | flops 4096 | bytes 32768 | tf_op jit(solution)/shard_map/psum | solution.py:89
  149.8 1.1 fusion.13
  153.0 1.9 copy.66
  154.9 1.3 fusion.10
  156.6 1.5 pad_maximum_fusion
  158.0 1.7 copy.70
  159.8 104.0 %while.12 = (s32[]{:T(128)}, f32[16,32,128]{2,1,0:T(8,128)S(1)}, s32[16,32,4]{1,0,2:T(8,128)}, f32[768,4,128]{0,2,1:T(8,128)S(1)}, f32[16,32,4,128]{3,2,1,0:T(4,128)S(1)}, /*index=5*/s32[]{:T(128)}) while((s32[]{:T(128)}, f32[16,32,128]{2,1,0:T(8,128)S(1)}, s32[16,32,4]{1,0,2:T(8,128)}, f32[768,4,128]{0,2,1:T(8,128)S(1)}, ...), condition=%wide.region_8.9_spmd, body=%wide.region_6.8_spmd.sunk | while | flops 627146752 | bytes 3606097 | solution.py:41
  160.6 1.0 fusion.63
  162.0 4.4 %multiply_reduce_fusion.2 = f32[32,128]{1,0:T(8,128)S(1)} fusion(f32[32,4,128]{2,1,0:T(4,128)S(1)} %copy.88, f32[32,128]{1,0:T(8,128)S(1)} %get-tuple-element.135, f32[32,4,128]{2,1,0:T(4,128)S(1)} %copy.90, f32[32,128]{1,0:T(8,128)S(1)} %get-tuple-element.137, f32[32,4,128]{2,1,0:T(4,128)S(1)} %copy.91, f32[32,128]{1,0:T(8,128)S(1)} %get-tuple-element.139, ...), kind=kLoop, calls=%fused_computation.clone.1 | loop fusion | flops 23064576 | bytes 327680 | tf_op jit(solution)/shard_map/while/body/eval_jaxpr/reduce_sum | solution.py:28
  167.1 1.0 fusion.63
  168.4 4.4 %multiply_reduce_fusion.2 = f32[32,128]{1,0:T(8,128)S(1)} fusion(f32[32,4,128]{2,1,0:T(4,128)S(1)} %copy.88, f32[32,128]{1,0:T(8,128)S(1)} %get-tuple-element.135, f32[32,4,128]{2,1,0:T(4,128)S(1)} %copy.90, f32[32,128]{1,0:T(8,128)S(1)} %get-tuple-element.137, f32[32,4,128]{2,1,0:T(4,128)S(1)} %copy.91, f32[32,128]{1,0:T(8,128)S(1)} %get-tuple-element.139, ...), kind=kLoop, calls=%fused_computation.clone.1 | loop fusion | flops 23064576 | bytes 327680 | tf_op jit(solution)/shard_map/while/body/eval_jaxpr/reduce_sum | solution.py:28
  173.6 1.0 fusion.63
  174.9 4.4 %multiply_reduce_fusion.2 = f32[32,128]{1,0:T(8,128)S(1)} fusion(f32[32,4,128]{2,1,0:T(4,128)S(1)} %copy.88, f32[32,128]{1,0:T(8,128)S(1)} %get-tuple-element.135, f32[32,4,128]{2,1,0:T(4,128)S(1)} %copy.90, f32[32,128]{1,0:T(8,128)S(1)} %get-tuple-element.137, f32[32,4,128]{2,1,0:T(4,128)S(1)} %copy.91, f32[32,128]{1,0:T(8,128)S(1)} %get-tuple-element.139, ...), kind=kLoop, calls=%fused_computation.clone.1 | loop fusion | flops 23064576 | bytes 327680 | tf_op jit(solution)/shard_map/while/body/eval_jaxpr/reduce_sum | solution.py:28
  180.1 1.0 fusion.63
  181.4 4.4 %multiply_reduce_fusion.2 = f32[32,128]{1,0:T(8,128)S(1)} fusion(f32[32,4,128]{2,1,0:T(4,128)S(1)} %copy.88, f32[32,128]{1,0:T(8,128)S(1)} %get-tuple-element.135, f32[32,4,128]{2,1,0:T(4,128)S(1)} %copy.90, f32[32,128]{1,0:T(8,128)S(1)} %get-tuple-element.137, f32[32,4,128]{2,1,0:T(4,128)S(1)} %copy.91, f32[32,128]{1,0:T(8,128)S(1)} %get-tuple-element.139, ...), kind=kLoop, calls=%fused_computation.clone.1 | loop fusion | flops 23064576 | bytes 327680 | tf_op jit(solution)/shard_map/while/body/eval_jaxpr/reduce_sum | solution.py:28
  186.6 1.0 fusion.63
  187.9 4.4 %multiply_reduce_fusion.2 = f32[32,128]{1,0:T(8,128)S(1)} fusion(f32[32,4,128]{2,1,0:T(4,128)S(1)} %copy.88, f32[32,128]{1,0:T(8,128)S(1)} %get-tuple-element.135, f32[32,4,128]{2,1,0:T(4,128)S(1)} %copy.90, f32[32,128]{1,0:T(8,128)S(1)} %get-tuple-element.137, f32[32,4,128]{2,1,0:T(4,128)S(1)} %copy.91, f32[32,128]{1,0:T(8,128)S(1)} %get-tuple-element.139, ...), kind=kLoop, calls=%fused_computation.clone.1 | loop fusion | flops 23064576 | bytes 327680 | tf_op jit(solution)/shard_map/while/body/eval_jaxpr/reduce_sum | solution.py:28
  193.1 1.0 fusion.63
  194.4 4.4 %multiply_reduce_fusion.2 = f32[32,128]{1,0:T(8,128)S(1)} fusion(f32[32,4,128]{2,1,0:T(4,128)S(1)} %copy.88, f32[32,128]{1,0:T(8,128)S(1)} %get-tuple-element.135, f32[32,4,128]{2,1,0:T(4,128)S(1)} %copy.90, f32[32,128]{1,0:T(8,128)S(1)} %get-tuple-element.137, f32[32,4,128]{2,1,0:T(4,128)S(1)} %copy.91, f32[32,128]{1,0:T(8,128)S(1)} %get-tuple-element.139, ...), kind=kLoop, calls=%fused_computation.clone.1 | loop fusion | flops 23064576 | bytes 327680 | tf_op jit(solution)/shard_map/while/body/eval_jaxpr/reduce_sum | solution.py:28
  199.6 1.0 fusion.63
  200.9 4.4 %multiply_reduce_fusion.2 = f32[32,128]{1,0:T(8,128)S(1)} fusion(f32[32,4,128]{2,1,0:T(4,128)S(1)} %copy.88, f32[32,128]{1,0:T(8,128)S(1)} %get-tuple-element.135, f32[32,4,128]{2,1,0:T(4,128)S(1)} %copy.90, f32[32,128]{1,0:T(8,128)S(1)} %get-tuple-element.137, f32[32,4,128]{2,1,0:T(4,128)S(1)} %copy.91, f32[32,128]{1,0:T(8,128)S(1)} %get-tuple-element.139, ...), kind=kLoop, calls=%fused_computation.clone.1 | loop fusion | flops 23064576 | bytes 327680 | tf_op jit(solution)/shard_map/while/body/eval_jaxpr/reduce_sum | solution.py:28
  206.1 1.0 fusion.63
  207.4 4.4 %multiply_reduce_fusion.2 = f32[32,128]{1,0:T(8,128)S(1)} fusion(f32[32,4,128]{2,1,0:T(4,128)S(1)} %copy.88, f32[32,128]{1,0:T(8,128)S(1)} %get-tuple-element.135, f32[32,4,128]{2,1,0:T(4,128)S(1)} %copy.90, f32[32,128]{1,0:T(8,128)S(1)} %get-tuple-element.137, f32[32,4,128]{2,1,0:T(4,128)S(1)} %copy.91, f32[32,128]{1,0:T(8,128)S(1)} %get-tuple-element.139, ...), kind=kLoop, calls=%fused_computation.clone.1 | loop fusion | flops 23064576 | bytes 327680 | tf_op jit(solution)/shard_map/while/body/eval_jaxpr/reduce_sum | solution.py:28
  212.6 1.0 fusion.63
  213.9 4.4 %multiply_reduce_fusion.2 = f32[32,128]{1,0:T(8,128)S(1)} fusion(f32[32,4,128]{2,1,0:T(4,128)S(1)} %copy.88, f32[32,128]{1,0:T(8,128)S(1)} %get-tuple-element.135, f32[32,4,128]{2,1,0:T(4,128)S(1)} %copy.90, f32[32,128]{1,0:T(8,128)S(1)} %get-tuple-element.137, f32[32,4,128]{2,1,0:T(4,128)S(1)} %copy.91, f32[32,128]{1,0:T(8,128)S(1)} %get-tuple-element.139, ...), kind=kLoop, calls=%fused_computation.clone.1 | loop fusion | flops 23064576 | bytes 327680 | tf_op jit(solution)/shard_map/while/body/eval_jaxpr/reduce_sum | solution.py:28
  219.0 1.0 fusion.63
  220.4 4.4 %multiply_reduce_fusion.2 = f32[32,128]{1,0:T(8,128)S(1)} fusion(f32[32,4,128]{2,1,0:T(4,128)S(1)} %copy.88, f32[32,128]{1,0:T(8,128)S(1)} %get-tuple-element.135, f32[32,4,128]{2,1,0:T(4,128)S(1)} %copy.90, f32[32,128]{1,0:T(8,128)S(1)} %get-tuple-element.137, f32[32,4,128]{2,1,0:T(4,128)S(1)} %copy.91, f32[32,128]{1,0:T(8,128)S(1)} %get-tuple-element.139, ...), kind=kLoop, calls=%fused_computation.clone.1 | loop fusion | flops 23064576 | bytes 327680 | tf_op jit(solution)/shard_map/while/body/eval_jaxpr/reduce_sum | solution.py:28
  226.9 4.4 %multiply_reduce_fusion.2 = f32[32,128]{1,0:T(8,128)S(1)} fusion(f32[32,4,128]{2,1,0:T(4,128)S(1)} %copy.88, f32[32,128]{1,0:T(8,128)S(1)} %get-tuple-element.135, f32[32,4,128]{2,1,0:T(4,128)S(1)} %copy.90, f32[32,128]{1,0:T(8,128)S(1)} %get-tuple-element.137, f32[32,4,128]{2,1,0:T(4,128)S(1)} %copy.91, f32[32,128]{1,0:T(8,128)S(1)} %get-tuple-element.139, ...), kind=kLoop, calls=%fused_computation.clone.1 | loop fusion | flops 23064576 | bytes 327680 | tf_op jit(solution)/shard_map/while/body/eval_jaxpr/reduce_sum | solution.py:28
  232.0 1.0 fusion.63
  233.4 4.4 %multiply_reduce_fusion.2 = f32[32,128]{1,0:T(8,128)S(1)} fusion(f32[32,4,128]{2,1,0:T(4,128)S(1)} %copy.88, f32[32,128]{1,0:T(8,128)S(1)} %get-tuple-element.135, f32[32,4,128]{2,1,0:T(4,128)S(1)} %copy.90, f32[32,128]{1,0:T(8,128)S(1)} %get-tuple-element.137, f32[32,4,128]{2,1,0:T(4,128)S(1)} %copy.91, f32[32,128]{1,0:T(8,128)S(1)} %get-tuple-element.139, ...), kind=kLoop, calls=%fused_computation.clone.1 | loop fusion | flops 23064576 | bytes 327680 | tf_op jit(solution)/shard_map/while/body/eval_jaxpr/reduce_sum | solution.py:28
  238.5 1.0 fusion.63
  239.9 4.4 %multiply_reduce_fusion.2 = f32[32,128]{1,0:T(8,128)S(1)} fusion(f32[32,4,128]{2,1,0:T(4,128)S(1)} %copy.88, f32[32,128]{1,0:T(8,128)S(1)} %get-tuple-element.135, f32[32,4,128]{2,1,0:T(4,128)S(1)} %copy.90, f32[32,128]{1,0:T(8,128)S(1)} %get-tuple-element.137, f32[32,4,128]{2,1,0:T(4,128)S(1)} %copy.91, f32[32,128]{1,0:T(8,128)S(1)} %get-tuple-element.139, ...), kind=kLoop, calls=%fused_computation.clone.1 | loop fusion | flops 23064576 | bytes 327680 | tf_op jit(solution)/shard_map/while/body/eval_jaxpr/reduce_sum | solution.py:28
  245.0 1.0 fusion.63
  246.4 4.4 %multiply_reduce_fusion.2 = f32[32,128]{1,0:T(8,128)S(1)} fusion(f32[32,4,128]{2,1,0:T(4,128)S(1)} %copy.88, f32[32,128]{1,0:T(8,128)S(1)} %get-tuple-element.135, f32[32,4,128]{2,1,0:T(4,128)S(1)} %copy.90, f32[32,128]{1,0:T(8,128)S(1)} %get-tuple-element.137, f32[32,4,128]{2,1,0:T(4,128)S(1)} %copy.91, f32[32,128]{1,0:T(8,128)S(1)} %get-tuple-element.139, ...), kind=kLoop, calls=%fused_computation.clone.1 | loop fusion | flops 23064576 | bytes 327680 | tf_op jit(solution)/shard_map/while/body/eval_jaxpr/reduce_sum | solution.py:28
  251.5 1.0 fusion.63
  252.9 4.4 %multiply_reduce_fusion.2 = f32[32,128]{1,0:T(8,128)S(1)} fusion(f32[32,4,128]{2,1,0:T(4,128)S(1)} %copy.88, f32[32,128]{1,0:T(8,128)S(1)} %get-tuple-element.135, f32[32,4,128]{2,1,0:T(4,128)S(1)} %copy.90, f32[32,128]{1,0:T(8,128)S(1)} %get-tuple-element.137, f32[32,4,128]{2,1,0:T(4,128)S(1)} %copy.91, f32[32,128]{1,0:T(8,128)S(1)} %get-tuple-element.139, ...), kind=kLoop, calls=%fused_computation.clone.1 | loop fusion | flops 23064576 | bytes 327680 | tf_op jit(solution)/shard_map/while/body/eval_jaxpr/reduce_sum | solution.py:28
  258.0 1.0 fusion.63
  259.3 4.4 %multiply_reduce_fusion.2 = f32[32,128]{1,0:T(8,128)S(1)} fusion(f32[32,4,128]{2,1,0:T(4,128)S(1)} %copy.88, f32[32,128]{1,0:T(8,128)S(1)} %get-tuple-element.135, f32[32,4,128]{2,1,0:T(4,128)S(1)} %copy.90, f32[32,128]{1,0:T(8,128)S(1)} %get-tuple-element.137, f32[32,4,128]{2,1,0:T(4,128)S(1)} %copy.91, f32[32,128]{1,0:T(8,128)S(1)} %get-tuple-element.139, ...), kind=kLoop, calls=%fused_computation.clone.1 | loop fusion | flops 23064576 | bytes 327680 | tf_op jit(solution)/shard_map/while/body/eval_jaxpr/reduce_sum | solution.py:28
  264.5 3.5 all-to-all-start.2
  268.0 1.4 fusion.14
  269.7 75.6 %psum.23 = f32[1024]{0:T(1024)S(1)} all-reduce(f32[1024]{0:T(1024)S(1)} %bitcast.156), channel_id=1, replica_groups=mesh['dom'=16,'grp'=16] {'dom','grp'}, use_global_device_ids=true, to_apply=%region_9.10 | all-reduce | flops 1024 | bytes 8192 | tf_op jit(solution)/shard_map/psum | solution.py:97
  345.9 1.3 convolution_add_fusion
  (226 shorter events, 27.6 us)
Async XLA Ops:
  12.9 24.1 %copy-start.11 = (s32[1,16]{1,0:T(1,128)S(1)}, s32[1,16]{1,0:T(1,128)}, u32[]{:S(2)}) copy-start(s32[1,16]{1,0:T(1,128)} %param.18) | copy-start | bytes 196
  13.6 28.0 %copy-start.10 = (s32[1,64]{1,0:T(1,128)S(1)}, s32[1,64]{1,0:T(1,128)}, u32[]{:S(2)}) copy-start(s32[1,64]{1,0:T(1,128)} %param.16) | copy-start | bytes 772
  37.1 5.9 %copy-start = (f32[256,128]{1,0:T(8,128)S(1)}, f32[256,128]{1,0:T(8,128)}, u32[]{:S(2)}) copy-start(f32[256,128]{1,0:T(8,128)} %param.13) | copy-start | bytes 393220
  37.1 6.0 %copy-start.1 = (f32[256,3,128]{2,0,1:T(8,128)S(1)}, f32[256,3,128]{2,0,1:T(8,128)}, u32[]{:S(2)}) copy-start(f32[256,3,128]{2,0,1:T(8,128)} %param.12) | copy-start | bytes 1179652
  37.7 114.7 %all-to-all-start.1 = ((s32[16,1,16]{2,1,0:T(1,128)}), s32[16,1,16]{2,1,0:T(1,128)S(1)}, u32[]{:S(2)}, u32[]{:S(2)}) async-start(s32[16,1,16]{2,1,0:T(1,128)} %stack.2), calls=%async_computation.1 | async-start | bytes 16384 | tf_op jit(solution)/shard_map/all_to_all | solution.py:119
  41.2 2.2 copy-start.3
  41.2 111.8 %all-gather.2.cloned.1.call-start = ((), (), s32[]{:S(2)}) async-start(), calls=%async_computation.3 | async-start | bytes 2228224 | tf_op jit(solution)/shard_map/all_gather | solution.py:115
  41.6 3.8 %copy-start.6 = (s32[1,16,16]{2,1,0:T(8,128)S(1)}, s32[1,16,16]{2,1,0:T(8,128)}, u32[]{:S(2)}) copy-start(s32[1,16,16]{2,1,0:T(8,128)} %param.17) | copy-start | bytes 3076
  43.4 108.3 %copy-start.7 = (s32[512,4]{0,1:T(4,128)S(1)}, s32[512,4]{0,1:T(4,128)}, u32[]{:S(2)}) copy-start(s32[512,4]{0,1:T(4,128)} %param.19) | copy-start | bytes 24580
  43.4 109.5 %copy-start.12 = (s32[16]{0:T(128)}, s32[16]{0:T(128)S(1)}, u32[]{:S(2)}) copy-start(s32[16]{0:T(128)S(1)} %and_select_fusion) | copy-start | bytes 196
  43.5 109.4 %copy-start.4 = (s32[32768]{0:T(1024)}, s32[32768]{0:T(1024)S(1)}, u32[]{:S(2)}) copy-start(s32[32768]{0:T(1024)S(1)} %add_select_fusion) | copy-start | bytes 393220
  149.6 3.3 copy-start.8
  159.7 108.3 %copy-start.2 = (f32[32768]{0:T(1024)S(1)}, f32[32768]{0:T(1024)}, u32[]{:S(2)}) copy-start(f32[32768]{0:T(1024)} %multiply_multiply_fusion) | copy-start | bytes 393220
  159.8 108.3 %copy-start.5 = (s32[32768]{0:T(1024)S(1)}, s32[32768]{0:T(1024)}, u32[]{:S(2)}) copy-start(s32[32768]{0:T(1024)} %copy-done.4) | copy-start | bytes 393220
  159.8 109.7 %copy-start.13 = (s32[16]{0:T(128)S(1)}, s32[16]{0:T(128)}, u32[]{:S(2)}) copy-start(s32[16]{0:T(128)} %copy-done.12) | copy-start | bytes 196
  159.8 185.5 %copy-start.9 = (f32[1024]{0:T(1024)S(1)}, f32[1024]{0:T(1024)}, u32[]{:S(2)}) copy-start(f32[1024]{0:T(1024)} %copy-done.8) | copy-start | bytes 12292
  264.5 81.4 %all-to-all-start.2 = ((f32[16,32,128]{2,1,0:T(8,128)}), f32[16,32,128]{2,1,0:T(8,128)S(1)}, u32[]{:S(2)}, u32[]{:S(2)}) async-start(f32[16,32,128]{2,1,0:T(8,128)} %broadcast_multiply_fusion), calls=%async_computation.2 | async-start | bytes 524288 | tf_op jit(solution)/shard_map/all_to_all | solution.py:133
Sparse Core Ops, SparseCore 0:
  45.0 53.1 all-gather.1
